TPU v7x, 512 devices: a whole 4x4x16 slice. The times are simulated.
512 devices in a mesh: ctx: 16 (over z_lo, y), ch: 32 (over z_hi, x, core).
Axes of the slice: x: 4, y: 4, z: 16 (z_hi: 4, z_lo: 4; z = z_hi * 4 + z_lo), core: 2. Of those that a mesh axis runs over, the one named last changes fastest.
Arguments:
- bases_in: bfloat16 [6144, 4096], P('ctx', 'ch'), may hold values from -70 to 70
- norm_gain: float32 [4096], replicated, may hold values from 0.1 to 1.9
- w_in: bfloat16 [4096, 3, 4096], P(None, None, 'ch'), may hold values from -0.09375 to 0.09375
- feat_taps: float32 [3, 3, 4096], P(None, None, 'ch'), may hold values from -3.5 to 3.5
- long_filter: bfloat16 [4096, 128], P('ch'), may hold values from -0.5 to 0.5
- skip_gain: float32 [4096], P('ch'), may hold values from -4 to 4
- w_out: bfloat16 [4096, 4096], P('ch'), may hold values from -0.1875 to 0.1875
Outputs:
- mixed: bfloat16 [6144, 4096], P('ctx', 'ch')
All inputs are finite; a program needn't handle non-finite values.
Results may differ from a plain program's by a relative error of at most 0.02.
Values may be sent and summed in bfloat16 or wider, within the bound.
No kernel may reach another device: no remote copies, remote signals or barrier semaphores. Data moves between devices by JAX's collectives and lax.ppermute only.
A program may use at most 128 MiB of HBM per device.

v0:
```python
import jax
import jax.numpy as jnp
from jax import lax
from jax.sharding import PartitionSpec as P


def passed_along(value, axis, steps):
    count = lax.axis_size(axis)
    initial, last = (max(0, -steps), min(count, count - steps))
    return lax.ppermute(value, axis, [(source, source + steps) for source in range(initial, last)])


def featurize(extended, feat_taps, count):
    feat_len = feat_taps.shape[1]
    chans = feat_taps.shape[2]
    shaped = extended.reshape(extended.shape[0], 3, chans)
    feats = jnp.zeros((count, 3, chans), jnp.float32)
    for tap in range(feat_len):
        feats = feats + feat_taps[:, tap, :] * shaped[
            feat_len - 1 - tap : feat_len - 1 - tap + count
        ].astype(jnp.float32)
    return feats


def band_matrix(long_filter):
    chans, taps = long_filter.shape
    row_len = 3 * taps - 1
    reversed_taps = long_filter[:, ::-1]
    padded_row = jnp.concatenate(
        [
            jnp.zeros((chans, taps), jnp.bfloat16),
            reversed_taps,
            jnp.zeros((chans, taps - 1), jnp.bfloat16),
        ],
        axis=1,
    )
    tiled = jnp.broadcast_to(padded_row[:, None, :], (chans, taps, row_len)).reshape(
        chans, taps * row_len
    )
    skewed = tiled[:, taps - 1 : taps - 1 + taps * (row_len - 1)].reshape(chans, taps, row_len - 1)
    return skewed[:, :, : 2 * taps]


def shards(bases_in, norm_gain, w_in, feat_taps, long_filter, skip_gain, w_out):
    tok, chans = bases_in.shape
    width = norm_gain.shape[0]
    taps = long_filter.shape[1]
    feat_len = feat_taps.shape[1]
    w_flat = w_in.reshape(width, 3 * chans)
    whole = lax.all_gather(bases_in, "ch", axis=1, tiled=True)
    wide = whole.astype(jnp.float32)
    inverse = lax.rsqrt(jnp.mean(wide * wide, axis=1, keepdims=True) + 1e-05)
    normed = (wide * inverse * norm_gain).astype(jnp.bfloat16)
    mixed_in = jnp.dot(normed, w_flat, preferred_element_type=jnp.float32)
    projected = mixed_in.astype(jnp.bfloat16)
    earlier = passed_along(projected[tok - (feat_len - 1) :], "ctx", 1)
    feats = featurize(jnp.concatenate([earlier, projected], axis=0), feat_taps, tok)
    query = feats[:, 0, :]
    product = (feats[:, 1, :] * feats[:, 2, :]).astype(jnp.bfloat16)
    before = passed_along(product[tok - (taps - 1) :], "ctx", 1)
    extended = jnp.concatenate([jnp.zeros((1, chans), jnp.bfloat16), before, product], axis=0)
    toeplitz = band_matrix(long_filter)
    blocks = tok // taps
    older = extended[:tok].reshape(blocks, taps, chans)
    newer = extended[taps:].reshape(blocks, taps, chans)
    window = jnp.concatenate([older, newer], axis=1)
    filtered = jnp.einsum(
        "cij,bjc->bic", toeplitz, window, preferred_element_type=jnp.float32
    ).reshape(tok, chans)
    gated = (query * (filtered + skip_gain * product.astype(jnp.float32))).astype(jnp.bfloat16)
    terms = jnp.dot(gated, w_out, preferred_element_type=jnp.float32)
    return lax.psum_scatter(terms.astype(jnp.bfloat16), "ch", scatter_dimension=1, tiled=True)


def solution(mesh):
    in_specs = (
        P("ctx", "ch"),
        P(),
        P(None, None, "ch"),
        P(None, None, "ch"),
        P("ch", None),
        P("ch"),
        P("ch", None),
    )
    out_specs = P("ctx", "ch")
    return jax.shard_map(shards, mesh=mesh, in_specs=in_specs, out_specs=out_specs, check_vma=False)
```

profile of v0, /device:TPU:1, one launch (start us, length us, event | category | flops | bytes accessed | tf_op | source)
XLA Modules:
  0.0 345.5 jit_solution(9485300635172362352)
XLA Ops:
  6.5 0.7 all-gather.2.cloned.1.call-update
  7.3 0.0 reduce-scatter.4.cloned.1.call-start
  7.3 4.7 %copy.25 = bf16[4096,3,128]{0,2,1:T(8,128)(2,1)} copy(bf16[4096,3,128]{2,0,1:T(8,128)(2,1)} %param.9) | data formatting | bytes 6291456 | tf_op args[2]
  12.1 96.0 %all-gather.2.cloned.1.call-done = bf16[384,4096]{1,0:T(8,128)(2,1)} async-done(((bf16[384,128]{1,0:T(8,128)(2,1)}), bf16[384,4096]{1,0:T(8,128)(2,1)}) %all-gather.2.cloned.1.call-update) | async-done | bytes 3145744 | tf_op jit(solution)/shard_map/all_gather | solution.py:50
  108.1 2.6 fusion.2
  110.7 4.7 %fusion.9 = bf16[384,384]{1,0:T(8,128)(2,1)S(1)} fusion(bf16[4096,384]{0,1:T(8,128)(2,1)} %bitcast.38, bf16[384,4096]{1,0:T(8,128)(2,1)} %all-gather.2.cloned.1.call-done, f32[4096]{0:T(1024)S(1)} %copy-done.4, f32[384]{0:T(512)S(1)} %add_rsqrt_fusion), kind=kOutput, calls=%fused_computation.11 | convolution fusion | flops 1214398464 | bytes 6604288 | tf_op jit(solution)/shard_map/dot_general | solution.py:54
  115.4 2.9 collective-permute-start
  118.3 0.1 rev.3
  118.5 0.2 copy.26
  118.6 0.4 collective-permute-done
  119.0 0.1 fusion.16
  119.1 0.2 copy.28
  119.3 0.2 copy.27
  119.6 0.2 multiply_add_fusion
  119.8 0.1 slice_bitcast_fusion.1
  119.9 3.6 %collective-permute-start.1 = (bf16[127,128]{0,1:T(8,128)(2,1)S(1)}, bf16[127,128]{0,1:T(8,128)(2,1)S(1)}, u32[]{:S(2)}, u32[]{:S(2)}) collective-permute-start(bf16[127,128]{0,1:T(8,128)(2,1)S(1)} %slice_bitcast_fusion.1), channel_id=1, source_target_pairs={{0,32},{32,64},{64,96},{96,128},{128,160},{160,192},{192,224},{224... | collective-permute-start | bytes 97544 | tf_op jit(solution)/shard_map/ppermute | solution.py:10
  123.6 5.6 %broadcast_in_dim.21 = bf16[128,128,383]{2,1,0:T(8,128)(2,1)} broadcast(bf16[128,383]{1,0:T(8,128)(2,1)S(1)} %maximum_maximum_fusion), dimensions={0,2} | broadcast | bytes 12648192 | tf_op jit(solution)/shard_map/broadcast_in_dim | solution.py:37
  129.2 22.9 %reshape.49 = bf16[128,49024]{1,0:T(8,128)(2,1)} reshape(bf16[128,128,383]{2,1,0:T(8,128)(2,1)} %broadcast_in_dim.21) | data formatting | bytes 25100288 | tf_op jit(solution)/shard_map/reshape | solution.py:37
  152.1 11.6 %slice.68 = bf16[128,48896]{1,0:T(8,128)(2,1)} slice(bf16[128,49024]{1,0:T(8,128)(2,1)} %reshape.49), slice={[0:128], [127:49023]} | slice | bytes 25034752 | tf_op jit(solution)/shard_map/slice | solution.py:40
  163.8 33.8 %reshape.50 = bf16[128,128,382]{2,1,0:T(8,128)(2,1)} reshape(bf16[128,48896]{1,0:T(8,128)(2,1)} %slice.68) | data formatting | bytes 25034752 | tf_op jit(solution)/shard_map/reshape | solution.py:40
  197.6 0.1 copy.29
  197.7 0.1 copy.33
  197.9 0.1 copy.30
  198.0 0.1 pad_maximum_fusion.1
  198.1 0.1 copy.32
  198.3 5.6 %fusion.12 = f32[3,128,128]{1,0,2:T(4,128)S(1)} fusion(bf16[128,128,382]{2,1,0:T(8,128)(2,1)} %reshape.50, bf16[3,128,128]{1,0,2:T(4,128)(2,1)S(1)} %copy.33, bf16[3,128,128]{1,0,2:T(4,128)(2,1)S(1)} %copy.32), kind=kOutput, calls=%fused_computation.12 | convolution fusion | flops 25559040 | bytes 8781824 | tf_op jit(solution)/shard_map/cij,bjc->bic/dot_general | solution.py:67
  203.9 0.1 copy.34
  204.1 0.1 copy.36
  204.2 2.8 convolution_convert_fusion
  207.0 4.6 %copy.38 = bf16[384,4096]{0,1:T(8,128)(2,1)} copy(bf16[384,4096]{1,0:T(8,128)(2,1)} %convolution_convert_fusion) | data formatting | bytes 6291456
  211.7 125.4 %reduce-scatter.4.cloned.1.call-done = bf16[128,384]{1,0:T(8,128)(2,1)} async-done(((bf16[4096,384]{1,0:T(8,128)(2,1)}), bf16[128,384]{1,0:T(8,128)(2,1)}) %reduce-scatter.4.cloned.1.call-update) | async-done | bytes 98320
  337.0 1.6 copy.39
  (25 shorter events, 0.1 us)
Async XLA Ops:
  6.5 197.7 %copy-start = (bf16[128,4096]{1,0:T(8,128)(2,1)S(1)}, bf16[128,4096]{1,0:T(8,128)(2,1)}, u32[]{:S(2)}) copy-start(bf16[128,4096]{1,0:T(8,128)(2,1)} %param.13) | copy-start | bytes 3145732
  6.5 5.5 %copy-start.2 = (f32[3,3,128]{2,1,0:T(4,128)S(1)}, f32[3,3,128]{2,1,0:T(4,128)}, u32[]{:S(2)}) copy-start(f32[3,3,128]{2,1,0:T(4,128)} %param.10) | copy-start | bytes 13828
  6.5 104.1 %copy-start.4 = (f32[4096]{0:T(1024)S(1)}, f32[4096]{0:T(1024)}, u32[]{:S(2)}) copy-start(f32[4096]{0:T(1024)} %param.8) | copy-start | bytes 49156
  6.5 101.5 %all-gather.2.cloned.1.call-start = ((), (), s32[]{:S(2)}) async-start(), calls=%async_computation.1 | async-start | bytes 3244032 | tf_op jit(solution)/shard_map/all_gather | solution.py:50
  7.3 329.8 %reduce-scatter.4.cloned.1.call-start = ((), (), s32[]{:S(2)}) async-start(), calls=%async_computation.2 | async-start | bytes 3244032
  110.7 7.7 %copy-start.1 = (bf16[128,128]{1,0:T(8,128)(2,1)S(1)}, bf16[128,128]{1,0:T(8,128)(2,1)}, u32[]{:S(2)}) copy-start(bf16[128,128]{1,0:T(8,128)(2,1)} %param.11) | copy-start | bytes 98308
  115.4 3.6 %collective-permute-start = (bf16[2,384]{1,0:T(2,128)(2,1)S(1)}, bf16[2,384]{1,0:T(2,128)(2,1)S(1)}, u32[]{:S(2)}, u32[]{:S(2)}) collective-permute-start(bf16[2,384]{1,0:T(2,128)(2,1)S(1)} %slice.60), channel_id=1, source_target_pairs={{0,32},{32,64},{64,96},{96,128},{128,160},{160,192},{192,224},{224... | collective-permute-start | bytes 4616 | tf_op jit(solution)/shard_map/ppermute | solution.py:10
  119.9 77.9 %collective-permute-start.1 = (bf16[127,128]{0,1:T(8,128)(2,1)S(1)}, bf16[127,128]{0,1:T(8,128)(2,1)S(1)}, u32[]{:S(2)}, u32[]{:S(2)}) collective-permute-start(bf16[127,128]{0,1:T(8,128)(2,1)S(1)} %slice_bitcast_fusion.1), channel_id=1, source_target_pairs={{0,32},{32,64},{64,96},{96,128},{128,160},{160,192},{192,224},{224... | collective-permute-start | bytes 97544 | tf_op jit(solution)/shard_map/ppermute | solution.py:10
  197.6 6.6 %copy-start.3 = (f32[128]{0:T(128)S(1)}, f32[128]{0:T(128)}, u32[]{:S(2)}) copy-start(f32[128]{0:T(128)} %param.12) | copy-start | bytes 1540
Sparse Core Ops, SparseCore 0:
  10.4 97.6 all-gather.1
  211.8 125.1 reduce-scatter.3
where the time goes:
time: 346 us; the launch traced here: 345 us
  waiting for transfers between devices  222 us (64%)
  local copies, waits for them, and re-layouts  86.7 us (25%)
  between operations  13.6 us (4%)
  matrix products  13.1 us (4%)
  starting transfers between devices  6.54 us (2%)
    unnamed x3, waiting for transfers between devices  126 us
    all_gather x1, waiting for transfers between devices, shards(): whole = lax.all_gather(bases_in, 'ch', axis=1, tiled=True)  96 us
    reshape x1, local copies, waits for them, and re-layouts, band_matrix(): tiled[:, taps - 1:taps - 1 + taps * (row_len - 1)]  33.8 us
    reshape x1, local copies, waits for them, and re-layouts, band_matrix(): jnp.broadcast_to(padded_row[:, None, :], (chans, taps, row_len))  22.9 us
    slice x1, local copies, waits for them, and re-layouts, band_matrix(): tiled[:, taps - 1:taps - 1 + taps * (row_len - 1)]  11.6 us
    unnamed x15, local copies, waits for them, and re-layouts  11 us
  transfers between devices with their start and end apart: 4, of which 3 were waited for; matrix products, arithmetic and copies ran while one was open for 23% of the time, Pallas kernels for 0%

commit v1 on v0

--- a/solution.py
+++ b/solution.py
@@ -47,7 +47,9 @@
     taps = long_filter.shape[1]
     feat_len = feat_taps.shape[1]
     w_flat = w_in.reshape(width, 3 * chans)
-    whole = lax.all_gather(bases_in, "ch", axis=1, tiled=True)
+    whole = jnp.concatenate(
+        lax.all_to_all(jnp.stack([bases_in] * lax.axis_size("ch")), "ch", 0, 0), axis=1
+    )
     wide = whole.astype(jnp.float32)
     inverse = lax.rsqrt(jnp.mean(wide * wide, axis=1, keepdims=True) + 1e-05)
     normed = (wide * inverse * norm_gain).astype(jnp.bfloat16)

time: 346 us -> 412 us (1.19)
  waiting for transfers between devices: 222 us -> 264 us
  starting transfers between devices: 6.54 us -> 26.3 us
    all_to_all x0 -> x1, waiting for transfers between devices: none -> 139 us  [shards(): lax.all_to_all(jnp.stack([bases_in] * lax.axis_size('ch')), 'ch', 0, 0)]
    all_gather x1 -> x0, waiting for transfers between devices: 96 us -> none  [shards(): whole = lax.all_gather(bases_in, 'ch', axis=1, tiled=True)]
    all_to_all x0 -> x1, starting transfers between devices: none -> 19.3 us  [shards(): lax.all_to_all(jnp.stack([bases_in] * lax.axis_size('ch')), 'ch', 0, 0)]
    unnamed x15 -> x18, local copies, waits for them, and re-layouts: 11 us -> 12.6 us
    unnamed x3 -> x2, waiting for transfers between devices: 126 us -> 125 us
  transfers between devices with their start and end apart: 4 -> 4, of which waited for: 3 -> 3; matrix products, arithmetic and copies ran while one was open for 23% -> 19% of each run, Pallas kernels for 0% -> 0%
where the time goes in v1:
time: 412 us; the launch traced here: 410 us
  waiting for transfers between devices  264 us (64%)
  local copies, waits for them, and re-layouts  90.4 us (22%)
  starting transfers between devices  26.3 us (6%)
  between operations  13.6 us (3%)
  matrix products  10.2 us (2%)
  other arithmetic  5.67 us (1%)
    all_to_all x1, waiting for transfers between devices, shards(): lax.all_to_all(jnp.stack([bases_in] * lax.axis_size('ch')), 'ch', 0, 0)  139 us
    unnamed x2, waiting for transfers between devices  125 us
    reshape x1, local copies, waits for them, and re-layouts, band_matrix(): tiled[:, taps - 1:taps - 1 + taps * (row_len - 1)]  33.8 us
    reshape x1, local copies, waits for them, and re-layouts, band_matrix(): jnp.broadcast_to(padded_row[:, None, :], (chans, taps, row_len))  22.9 us
    all_to_all x1, starting transfers between devices, shards(): lax.all_to_all(jnp.stack([bases_in] * lax.axis_size('ch')), 'ch', 0, 0)  19.3 us
    unnamed x18, local copies, waits for them, and re-layouts  12.6 us
    slice x1, local copies, waits for them, and re-layouts, band_matrix(): tiled[:, taps - 1:taps - 1 + taps * (row_len - 1)]  11.6 us
  transfers between devices with their start and end apart: 4, of which 3 were waited for; matrix products, arithmetic and copies ran while one was open for 19% of the time, Pallas kernels for 0%

profile of v1, /device:TPU:1, one launch (start us, length us, event | category | flops | bytes accessed | tf_op | source)
XLA Modules:
  0.0 410.4 jit_solution(1631463012941711661)
XLA Ops:
  6.5 1.1 copy.26
  7.6 2.2 stack.2
  9.8 19.3 %all-to-all-start = ((bf16[32,384,128]{1,2,0:T(8,128)(2,1)}), bf16[32,384,128]{1,2,0:T(8,128)(2,1)}, u32[]{:S(2)}, u32[]{:S(2)}) async-start(bf16[32,384,128]{1,2,0:T(8,128)(2,1)} %stack.2), calls=%async_computation | async-start | bytes 6291456 | tf_op jit(solution)/shard_map/all_to_all | solution.py:51
  29.1 4.9 %copy.27 = bf16[4096,3,128]{0,2,1:T(8,128)(2,1)} copy(bf16[4096,3,128]{2,0,1:T(8,128)(2,1)} %param.9) | data formatting | bytes 6291456 | tf_op args[2]
  34.0 139.0 %all-to-all-done = bf16[32,384,128]{1,2,0:T(8,128)(2,1)} async-done(((bf16[32,384,128]{1,2,0:T(8,128)(2,1)}), bf16[32,384,128]{1,2,0:T(8,128)(2,1)}, u32[]{:S(2)}, u32[]{:S(2)}) %all-to-all-start) | async-done | bytes 3145760 | tf_op jit(solution)/shard_map/all_to_all | solution.py:51
  173.0 2.7 fusion.2
  175.7 2.5 fusion.4
  178.2 0.3 copy-done.1
  178.6 1.8 convolution_convert_fusion.1
  180.4 3.2 collective-permute-start
  183.8 0.2 copy.28
  184.0 0.4 collective-permute-done
  184.4 0.2 copy.30
  184.7 0.2 copy.29
  184.9 0.2 multiply_add_fusion
  185.2 3.8 collective-permute-start.1
  189.1 5.6 %broadcast_in_dim.21 = bf16[128,128,383]{2,1,0:T(8,128)(2,1)} broadcast(bf16[128,383]{1,0:T(8,128)(2,1)S(1)} %maximum_maximum_fusion), dimensions={0,2} | broadcast | bytes 12648192 | tf_op jit(solution)/shard_map/broadcast_in_dim | solution.py:37
  194.7 22.9 %reshape.64 = bf16[128,49024]{1,0:T(8,128)(2,1)} reshape(bf16[128,128,383]{2,1,0:T(8,128)(2,1)} %broadcast_in_dim.21) | data formatting | bytes 25100288 | tf_op jit(solution)/shard_map/reshape | solution.py:37
  217.6 11.6 %slice.68 = bf16[128,48896]{1,0:T(8,128)(2,1)} slice(bf16[128,49024]{1,0:T(8,128)(2,1)} %reshape.64), slice={[0:128], [127:49023]} | slice | bytes 25034752 | tf_op jit(solution)/shard_map/slice | solution.py:40
  229.3 33.8 %reshape.65 = bf16[128,128,382]{2,1,0:T(8,128)(2,1)} reshape(bf16[128,48896]{1,0:T(8,128)(2,1)} %slice.68) | data formatting | bytes 25034752 | tf_op jit(solution)/shard_map/reshape | solution.py:40
  263.1 0.1 copy.31
  263.2 0.1 copy.35
  263.4 0.1 copy.32
  263.5 0.1 pad_maximum_fusion.1
  263.6 0.1 copy.34
  263.8 5.6 %fusion.5 = f32[3,128,128]{1,0,2:T(4,128)S(1)} fusion(bf16[128,128,382]{2,1,0:T(8,128)(2,1)} %reshape.65, bf16[3,128,128]{1,0,2:T(4,128)(2,1)S(1)} %copy.35, bf16[3,128,128]{1,0,2:T(4,128)(2,1)S(1)} %copy.34), kind=kOutput, calls=%fused_computation.9 | convolution fusion | flops 25559040 | bytes 8781824 | tf_op jit(solution)/shard_map/cij,bjc->bic/dot_general | solution.py:69
  269.4 0.1 copy.36
  269.6 0.1 copy.38
  269.7 2.8 convolution_convert_fusion
  272.5 4.6 %copy.40 = bf16[384,4096]{0,1:T(8,128)(2,1)} copy(bf16[384,4096]{1,0:T(8,128)(2,1)} %convolution_convert_fusion) | data formatting | bytes 6291456
  277.2 124.7 %reduce-scatter.4.cloned.1.call-done = bf16[128,384]{1,0:T(8,128)(2,1)} async-done(((bf16[4096,384]{1,0:T(8,128)(2,1)}), bf16[128,384]{1,0:T(8,128)(2,1)}) %reduce-scatter.4.cloned.1.call-update) | async-done | bytes 98320
  401.9 1.6 copy.41
  (29 shorter events, 0.5 us)
Async XLA Ops:
  6.5 263.2 %copy-start = (bf16[128,4096]{1,0:T(8,128)(2,1)S(1)}, bf16[128,4096]{1,0:T(8,128)(2,1)}, u32[]{:S(2)}) copy-start(bf16[128,4096]{1,0:T(8,128)(2,1)} %param.13) | copy-start | bytes 3145732
  9.8 163.2 %all-to-all-start = ((bf16[32,384,128]{1,2,0:T(8,128)(2,1)}), bf16[32,384,128]{1,2,0:T(8,128)(2,1)}, u32[]{:S(2)}, u32[]{:S(2)}) async-start(bf16[32,384,128]{1,2,0:T(8,128)(2,1)} %stack.2), calls=%async_computation | async-start | bytes 6291456 | tf_op jit(solution)/shard_map/all_to_all | solution.py:51
  29.1 4.9 %copy-start.4 = (f32[3,3,128]{2,1,0:T(4,128)S(1)}, f32[3,3,128]{2,1,0:T(4,128)}, u32[]{:S(2)}) copy-start(f32[3,3,128]{2,1,0:T(4,128)} %param.10) | copy-start | bytes 13828
  29.1 372.8 %reduce-scatter.4.cloned.1.call-start = ((), (), s32[]{:S(2)}) async-start(), calls=%async_computation.2 | async-start | bytes 3244032
  34.0 141.7 %copy-start.3 = (f32[4096]{0:T(1024)S(1)}, f32[4096]{0:T(1024)}, u32[]{:S(2)}) copy-start(f32[4096]{0:T(1024)} %param.8) | copy-start | bytes 49156
  175.7 2.8 copy-start.1
  178.6 5.1 %copy-start.2 = (bf16[128,128]{1,0:T(8,128)(2,1)S(1)}, bf16[128,128]{1,0:T(8,128)(2,1)}, u32[]{:S(2)}) copy-start(bf16[128,128]{1,0:T(8,128)(2,1)} %param.11) | copy-start | bytes 98308
  180.4 3.9 collective-permute-start
  185.2 78.1 %collective-permute-start.1 = (bf16[127,128]{0,1:T(8,128)(2,1)S(1)}, bf16[127,128]{0,1:T(8,128)(2,1)S(1)}, u32[]{:S(2)}, u32[]{:S(2)}) collective-permute-start(bf16[127,128]{0,1:T(8,128)(2,1)S(1)} %slice_bitcast_fusion.1), channel_id=1, source_target_pairs={{0,32},{32,64},{64,96},{96,128},{128,160},{160,192},{192,224},{224... | collective-permute-start | bytes 97544 | tf_op jit(solution)/shard_map/ppermute | solution.py:10
  263.8 6.0 %copy-start.5 = (f32[128]{0:T(128)S(1)}, f32[128]{0:T(128)}, u32[]{:S(2)}) copy-start(f32[128]{0:T(128)} %param.12) | copy-start | bytes 1540
Sparse Core Ops, SparseCore 0:
  277.3 124.5 reduce-scatter.3
